TPU v7x, 256 devices: a whole 4x4x8 slice. The times are simulated.
256 devices in a mesh: lon: 16 (over z, core), lat: 16 (over x, y).
Axes of the slice: x: 4, y: 4, z: 8, core: 2. Of those that a mesh axis runs over, the one named last changes fastest.
Arguments:
- state: float32 [16, 512, 4096], P(None, 'lat', 'lon'), may hold values from -6 to 6
- coef_lon: float32 [512, 4096], P('lat', 'lon'), may hold values from 0.2 to 0.24
- coef_lat: float32 [512, 4096], P('lat', 'lon'), may hold values from 0.2 to 0.24
- land_sea: int32 [512, 4096], P('lat', 'lon'), may hold values 0 or 1
- send_cols: int32 [16, 65536], P('lat', 'lon'), may hold values from 0 to 8191
- send_count: int32 [16, 256], P('lat', 'lon'), may hold values from 32 to 256, as said below
- obs_value: float32 [16, 16, 65536], P(None, 'lat', 'lon'), may hold values from -6 to 6
- obs_weight: float32 [16, 16, 65536], P(None, 'lat', 'lon'), may hold values from 0.25 to 4
Outputs:
- increment: float32 [16, 512, 4096], P(None, 'lat', 'lon')
Inputs may be any that keep to these rules, and one draw needn't show every extreme that they name: `send_count`: at most 256 live slots go from one device to one peer; in every latitude band some receiving device gets 256 from every device of the band, which one drawn from the seed. `send_cols`: entries index a column of the sending device's own block, row-major over its 32 x 256 cells.
All inputs are finite; a program needn't handle non-finite values. No bound on the sum of `land_sea` on one device may be relied on, other than what follows from the above.
Results may differ from a plain program's by a relative error of at most 0.00002.
Values sent between devices are 32-bit elements; how exact they have to be, the bound alone decides.
No kernel may reach another device: no remote copies, remote signals or barrier semaphores. Data moves between devices by JAX's collectives and lax.ppermute only.
A program may use at most 64 MiB of HBM per device.

v0:
```python
import jax
import jax.numpy as jnp
from jax import lax
from jax.sharding import PartitionSpec as P

PASSES = 8


def with_halo(block, sides, width):
    for axis, dim in sides:
        count = lax.axis_size(axis)
        forward = [(i, i + 1) for i in range(count - 1)]
        forward.append((count - 1, 0))
        backward = [(target, source) for source, target in forward]
        low = lax.ppermute(
            lax.slice_in_dim(block, block.shape[dim] - width, None, axis=dim), axis, forward
        )
        high = lax.ppermute(lax.slice_in_dim(block, 0, width, axis=dim), axis, backward)
        block = jnp.concatenate([low, block, high], axis=dim)
    return block


def one_pass(layer_field, east_face, north_face):
    flux_east = east_face * (layer_field[:, :, 1:] - layer_field[:, :, :-1])
    flux_north = north_face * (layer_field[:, 1:, :] - layer_field[:, :-1, :])
    return (
        layer_field[:, 1:-1, 1:-1]
        + flux_east[:, 1:-1, 1:]
        - flux_east[:, 1:-1, :-1]
        + flux_north[:, 1:, 1:-1]
        - flux_north[:, :-1, 1:-1]
    )


def body(state, coef_lon, coef_lat, land_sea, send_cols, send_count, obs_value, obs_weight):
    levels, rows_here, cols_here = state.shape
    lon_count = lax.axis_size("lon")
    lat_count = lax.axis_size("lat")
    slots = send_cols.shape[1]
    capacity = slots // lon_count
    columns = state.reshape(levels, rows_here * cols_here)
    targets = send_cols[0]
    slot_index = jnp.arange(slots, dtype=jnp.int32)
    limits = jnp.broadcast_to(send_count[0][:, None], (lon_count, capacity)).reshape(slots)
    usable = jnp.where(slot_index % capacity < limits, 1.0, 0.0).astype(jnp.float32)
    held = jnp.stack([obs_value[:, 0, :], obs_weight[:, 0, :]])
    at_owner = lax.all_to_all(held, "lon", split_axis=2, concat_axis=2, tiled=True)
    at_column = jnp.take(columns, targets, axis=1)
    weighted = at_owner[1] * (at_owner[0] - at_column) * usable
    sea = land_sea.astype(jnp.float32)
    gradient = jnp.zeros((levels, rows_here * cols_here), jnp.float32).at[:, targets].add(weighted)
    gradient = gradient.reshape(levels, rows_here, cols_here) * sea[None]
    rim_width = PASSES
    stacked = jnp.stack([sea, coef_lon, coef_lat])
    padded = with_halo(stacked, (("lon", 2), ("lat", 1)), rim_width)
    lat_index = lax.axis_index("lat")
    row_place = jnp.arange(rows_here + 2 * rim_width, dtype=jnp.int32)
    outside = (row_place < rim_width) & (lat_index == 0) | (row_place >= rows_here + rim_width) & (
        lat_index == lat_count - 1
    )
    inside = jnp.where(outside, 0.0, 1.0).astype(jnp.float32)[:, None]
    sea_rim = padded[0] * inside
    east_face = padded[1][:, :-1] * sea_rim[:, :-1] * sea_rim[:, 1:]
    north_face = padded[2][:-1, :] * sea_rim[:-1, :] * sea_rim[1:, :]
    field = with_halo(gradient, (("lon", 2), ("lat", 1)), rim_width)
    for step_number in range(PASSES):
        high, wide = (field.shape[1], field.shape[2])
        field = one_pass(
            field,
            east_face[step_number : step_number + high, step_number : step_number + wide - 1],
            north_face[step_number : step_number + high - 1, step_number : step_number + wide],
        )
    gradient = field
    return gradient


def solution(mesh):
    placed = (
        P(None, "lat", "lon"),
        P("lat", "lon"),
        P("lat", "lon"),
        P("lat", "lon"),
        P("lat", "lon"),
        P("lat", "lon"),
        P(None, "lat", "lon"),
        P(None, "lat", "lon"),
    )
    return jax.shard_map(
        body, mesh=mesh, in_specs=placed, out_specs=P(None, "lat", "lon"), check_vma=False
    )
```

profile of v0, /device:TPU:32, one launch (start us, length us, event | category | flops | bytes accessed | tf_op | source)
XLA Modules:
  0.0 152.6 jit_solution(4161188813281966988)
XLA Ops:
  0.0 1.3 copy_bitcast_fusion
  1.4 4.4 %copy.17 = f32[2,16,4096]{1,0,2:T(2,128)} copy(f32[2,16,4096]{2,1,0:T(8,128)S(1)} %pad_maximum_fusion.1) | data formatting | bytes 1048576 | tf_op jit(solution)/shard_map/stack | solution.py:46
  5.8 8.0 %reshape.116 = f32[16,1,8192]{2,1,0:T(1,128)} reshape(f32[4096,2,16]{2,1,0:T(2,128)} %bitcast.49) | data formatting | bytes 1048576
  13.7 8.7 %all-to-all-start = ((f32[16,1,8192]{2,1,0:T(1,128)}), f32[16,1,8192]{2,1,0:T(1,128)S(1)}, u32[]{:S(2)}, u32[]{:S(2)}) async-start(f32[16,1,8192]{2,1,0:T(1,128)} %reshape.116), calls=%async_computation | async-start | bytes 1048576 | tf_op jit(solution)/shard_map/all_to_all | solution.py:47
  22.7 0.4 collective-permute-start.4
  23.3 11.7 %collective-permute-done.5 = f32[3,32,8]{2,1,0:T(8,128)S(1)} collective-permute-done((f32[3,32,8]{2,1,0:T(8,128)S(1)}, f32[3,32,8]{2,1,0:T(8,128)S(1)}, u32[]{:S(2)}, u32[]{:S(2)}) %collective-permute-start.5) | collective-permute-done | bytes 3104 | tf_op jit(solution)/shard_map/ppermute | solution.py:18
  35.1 5.3 %collective-permute-start.7 = (f32[3,8,272]{2,1,0:T(8,128)S(1)}, f32[3,8,272]{2,1,0:T(8,128)S(1)}, u32[]{:S(2)}, u32[]{:S(2)}) collective-permute-start(f32[3,8,272]{2,1,0:T(8,128)S(1)} %get-tuple-element.12), channel_id=1, source_target_pairs={{1,0},{2,1},{3,2},{4,3},{5,4},{6,5},{7,6},{8,7},{9,8},{10,9},{11,1... | collective-permute-start | bytes 78344 | tf_op jit(solution)/shard_map/ppermute | solution.py:18
  40.4 2.6 %copy.20 = f32[16,32,256]{0,2,1:T(8,128)} copy(f32[16,32,256]{2,1,0:T(8,128)S(1)} %copy-done.1) | data formatting | bytes 1048576 | tf_op args[0]
  43.1 4.6 %collective-permute-done.6 = f32[3,8,272]{2,1,0:T(8,128)S(1)} collective-permute-done((f32[3,8,272]{2,1,0:T(8,128)S(1)}, f32[3,8,272]{2,1,0:T(8,128)S(1)}, u32[]{:S(2)}, u32[]{:S(2)}) %collective-permute-start.6) | collective-permute-done | bytes 26144 | tf_op jit(solution)/shard_map/ppermute | solution.py:15
  47.9 0.5 broadcast.109
  48.4 1.9 %reduce = f32[16,8192]{1,0:T(8,128)S(1)} reduce(f32[16,1,8192]{2,1,0:T(1,128)S(1)} %all-to-all-done, f32[]{:T(128)} %broadcast.109), dimensions={1}, to_apply=%all_to_all.3.reduce_sub_computation | reduce | bytes 1048580 | tf_op jit(solution)/shard_map/all_to_all | solution.py:47
  50.3 7.0 %reshape.117 = f32[4096,2,16]{2,1,0:T(2,128)} reshape(f32[16,8192]{1,0:T(8,128)S(1)} %reduce) | data formatting | bytes 1048576
  57.3 7.6 %fusion.33 = (f32[1,16,4096]{1,0,2:T(1,128)S(1)}, f32[1,16,4096]{1,0,2:T(1,128)}) fusion(f32[2,16,4096]{1,0,2:T(2,128)} %bitcast.52), kind=kLoop, calls=%fused_computation.114 | loop fusion | bytes 1048576 | tf_op jit(solution)/shard_map/slice | solution.py:49
  64.9 51.2 %scatter_custom_fusion = f32[16,8192]{0,1:T(8,128)} fusion(s32[4096]{0:T(1024)S(1)} %bitcast.63, f32[16,4096]{0,1:T(8,128)} %bitcast.54, f32[16,4096]{0,1:T(8,128)S(1)} %bitcast.53, f32[]{:T(128)} %constant.19.clone.1, f32[]{:T(128)} %constant.23.clone.1, f32[4096]{0:T(1024)S(1)} %fusion.31, pred[4096]{0:T(1024)(128)(4,1)S(1)} %compare_and_fusion, ...), kind=kCustom, calls=%fused_computation.2 | custom fusion | flops 327680 | bytes 3444744 | tf_op jit(solution)/shard_map/scatter-add | solution.py:51
  116.1 2.9 %copy.21 = f32[16,32,256]{2,1,0:T(8,128)S(1)} copy(f32[16,32,256]{0,2,1:T(8,128)} %bitcast.51) | data formatting | bytes 1048576 | tf_op jit(solution)/shard_map/reshape | solution.py:52
  119.2 0.8 collective-permute-start.1
  120.2 3.7 %collective-permute-done.1 = f32[16,32,8]{2,1,0:T(8,128)S(1)} collective-permute-done((f32[16,32,8]{2,1,0:T(8,128)S(1)}, f32[16,32,8]{2,1,0:T(8,128)S(1)}, u32[]{:S(2)}, u32[]{:S(2)}) %collective-permute-start.1) | collective-permute-done | bytes 16416 | tf_op jit(solution)/shard_map/ppermute | solution.py:18
  123.9 2.6 %collective-permute-done = f32[16,32,8]{2,1,0:T(8,128)S(1)} collective-permute-done((f32[16,32,8]{2,1,0:T(8,128)S(1)}, f32[16,32,8]{2,1,0:T(8,128)S(1)}, u32[]{:S(2)}, u32[]{:S(2)}) %collective-permute-start) | collective-permute-done | bytes 16416 | tf_op jit(solution)/shard_map/ppermute | solution.py:15
  126.5 0.2 pad_maximum_fusion.5
  126.7 0.9 collective-permute-start.3
  127.6 1.2 collective-permute-start.2
  129.9 3.0 %collective-permute-done.3 = f32[16,8,272]{2,1,0:T(8,128)S(1)} collective-permute-done((f32[16,8,272]{2,1,0:T(8,128)S(1)}, f32[16,8,272]{2,1,0:T(8,128)S(1)}, u32[]{:S(2)}, u32[]{:S(2)}) %collective-permute-start.3) | collective-permute-done | bytes 139296 | tf_op jit(solution)/shard_map/ppermute | solution.py:18
  132.9 4.6 %collective-permute-done.2 = f32[16,8,272]{2,1,0:T(8,128)S(1)} collective-permute-done((f32[16,8,272]{2,1,0:T(8,128)S(1)}, f32[16,8,272]{2,1,0:T(8,128)S(1)}, u32[]{:S(2)}, u32[]{:S(2)}) %collective-permute-start.2) | collective-permute-done | bytes 139296 | tf_op jit(solution)/shard_map/ppermute | solution.py:15
  137.5 0.3 pad_maximum_fusion
  137.9 0.2 fusion.13
  138.0 0.4 fusion.14
  138.4 1.4 slice_subtract_fusion.10
  139.9 0.2 fusion.11
  140.0 0.4 fusion.12
  140.4 1.4 slice_subtract_fusion.6
  141.9 0.2 fusion.9
  142.0 0.4 fusion.10
  142.4 1.4 slice_subtract_fusion.2
  143.9 0.2 fusion.7
  144.0 0.4 fusion.8
  144.4 1.2 slice_subtract_fusion.28
  145.6 0.1 fusion.24
  145.7 0.3 fusion.25
  146.1 1.2 slice_subtract_fusion.24
  147.3 0.1 fusion.22
  147.4 0.3 fusion.23
  147.8 1.2 slice_subtract_fusion.20
  149.0 0.1 fusion.20
  149.1 0.3 fusion.21
  149.4 1.2 slice_subtract_fusion.16
  150.6 0.1 fusion.18
  150.8 0.3 fusion.19
  151.1 1.5 slice_subtract_fusion.30
  (51 shorter events, 2.1 us)
Async XLA Ops:
  0.0 23.1 %copy-start = (s32[1,16]{1,0:T(1,128)S(1)}, s32[1,16]{1,0:T(1,128)}, u32[]{:S(2)}) copy-start(s32[1,16]{1,0:T(1,128)} %param.13) | copy-start | bytes 196
  5.8 16.7 %copy-start.5 = (s32[32,256]{1,0:T(8,128)S(1)}, s32[32,256]{1,0:T(8,128)}, u32[]{:S(2)}) copy-start(s32[32,256]{1,0:T(8,128)} %param.11) | copy-start | bytes 98308
  5.8 16.7 %copy-start.2 = (f32[32,256]{1,0:T(8,128)S(1)}, f32[32,256]{1,0:T(8,128)}, u32[]{:S(2)}) copy-start(f32[32,256]{1,0:T(8,128)} %param.10) | copy-start | bytes 98308
  5.8 16.7 %copy-start.3 = (f32[32,256]{1,0:T(8,128)S(1)}, f32[32,256]{1,0:T(8,128)}, u32[]{:S(2)}) copy-start(f32[32,256]{1,0:T(8,128)} %param.9) | copy-start | bytes 98308
  13.7 9.4 %copy-start.4 = (s32[1,4096]{1,0:T(1,128)S(1)}, s32[1,4096]{1,0:T(1,128)}, u32[]{:S(2)}) copy-start(s32[1,4096]{1,0:T(1,128)} %param.12) | copy-start | bytes 49156
  13.7 26.7 %copy-start.1 = (f32[16,32,256]{2,1,0:T(8,128)S(1)}, f32[16,32,256]{2,1,0:T(8,128)}, u32[]{:S(2)}) copy-start(f32[16,32,256]{2,1,0:T(8,128)} %param.8) | copy-start | bytes 1572868
  13.7 34.2 %all-to-all-start = ((f32[16,1,8192]{2,1,0:T(1,128)}), f32[16,1,8192]{2,1,0:T(1,128)S(1)}, u32[]{:S(2)}, u32[]{:S(2)}) async-start(f32[16,1,8192]{2,1,0:T(1,128)} %reshape.116), calls=%async_computation | async-start | bytes 1048576 | tf_op jit(solution)/shard_map/all_to_all | solution.py:47
  22.6 12.4 %collective-permute-start.5 = (f32[3,32,8]{2,1,0:T(8,128)S(1)}, f32[3,32,8]{2,1,0:T(8,128)S(1)}, u32[]{:S(2)}, u32[]{:S(2)}) collective-permute-start(f32[3,32,8]{2,1,0:T(8,128)S(1)} %get-tuple-element.14), channel_id=1, source_target_pairs={{16,0},{32,16},{48,32},{64,48},{80,64},{96,80},{112,96},{128,112},... | collective-permute-start | bytes 9224 | tf_op jit(solution)/shard_map/ppermute | solution.py:18
  22.7 12.3 %collective-permute-start.4 = (f32[3,32,8]{2,1,0:T(8,128)S(1)}, f32[3,32,8]{2,1,0:T(8,128)S(1)}, u32[]{:S(2)}, u32[]{:S(2)}) collective-permute-start(f32[3,32,8]{2,1,0:T(8,128)S(1)} %get-tuple-element.13), channel_id=1, source_target_pairs={{0,16},{16,32},{32,48},{48,64},{64,80},{80,96},{96,112},{112,128},... | collective-permute-start | bytes 9224 | tf_op jit(solution)/shard_map/ppermute | solution.py:15
  35.1 8.0 %collective-permute-start.7 = (f32[3,8,272]{2,1,0:T(8,128)S(1)}, f32[3,8,272]{2,1,0:T(8,128)S(1)}, u32[]{:S(2)}, u32[]{:S(2)}) collective-permute-start(f32[3,8,272]{2,1,0:T(8,128)S(1)} %get-tuple-element.12), channel_id=1, source_target_pairs={{1,0},{2,1},{3,2},{4,3},{5,4},{6,5},{7,6},{8,7},{9,8},{10,9},{11,1... | collective-permute-start | bytes 78344 | tf_op jit(solution)/shard_map/ppermute | solution.py:18
  40.4 7.3 %collective-permute-start.6 = (f32[3,8,272]{2,1,0:T(8,128)S(1)}, f32[3,8,272]{2,1,0:T(8,128)S(1)}, u32[]{:S(2)}, u32[]{:S(2)}) collective-permute-start(f32[3,8,272]{2,1,0:T(8,128)S(1)} %get-tuple-element.11), channel_id=1, source_target_pairs={{0,1},{1,2},{2,3},{3,4},{4,5},{5,6},{6,7},{7,8},{8,9},{9,10},{10,1... | collective-permute-start | bytes 78344 | tf_op jit(solution)/shard_map/ppermute | solution.py:15
  119.2 4.7 %collective-permute-start.1 = (f32[16,32,8]{2,1,0:T(8,128)S(1)}, f32[16,32,8]{2,1,0:T(8,128)S(1)}, u32[]{:S(2)}, u32[]{:S(2)}) collective-permute-start(f32[16,32,8]{2,1,0:T(8,128)S(1)} %get-tuple-element.10), channel_id=1, source_target_pairs={{16,0},{32,16},{48,32},{64,48},{80,64},{96,80},{112,96},{128,112},... | collective-permute-start | bytes 49160 | tf_op jit(solution)/shard_map/ppermute | solution.py:18
  120.0 6.5 %collective-permute-start = (f32[16,32,8]{2,1,0:T(8,128)S(1)}, f32[16,32,8]{2,1,0:T(8,128)S(1)}, u32[]{:S(2)}, u32[]{:S(2)}) collective-permute-start(f32[16,32,8]{2,1,0:T(8,128)S(1)} %get-tuple-element.9), channel_id=1, source_target_pairs={{0,16},{16,32},{32,48},{48,64},{64,80},{80,96},{96,112},{112,128},... | collective-permute-start | bytes 49160 | tf_op jit(solution)/shard_map/ppermute | solution.py:15
  126.7 6.2 %collective-permute-start.3 = (f32[16,8,272]{2,1,0:T(8,128)S(1)}, f32[16,8,272]{2,1,0:T(8,128)S(1)}, u32[]{:S(2)}, u32[]{:S(2)}) collective-permute-start(f32[16,8,272]{2,1,0:T(8,128)S(1)} %get-tuple-element.8), channel_id=1, source_target_pairs={{1,0},{2,1},{3,2},{4,3},{5,4},{6,5},{7,6},{8,7},{9,8},{10,9},{11,1... | collective-permute-start | bytes 417800 | tf_op jit(solution)/shard_map/ppermute | solution.py:18
  127.6 10.0 %collective-permute-start.2 = (f32[16,8,272]{2,1,0:T(8,128)S(1)}, f32[16,8,272]{2,1,0:T(8,128)S(1)}, u32[]{:S(2)}, u32[]{:S(2)}) collective-permute-start(f32[16,8,272]{2,1,0:T(8,128)S(1)} %get-tuple-element.7), channel_id=1, source_target_pairs={{0,1},{1,2},{2,3},{3,4},{4,5},{5,6},{6,7},{7,8},{8,9},{9,10},{10,1... | collective-permute-start | bytes 417800 | tf_op jit(solution)/shard_map/ppermute | solution.py:15
where the time goes:
time: 153 us
  other arithmetic  68.8 us (45%)
  local copies, waits for them, and re-layouts  35.8 us (23%)
  waiting for transfers between devices  30.2 us (20%)
  starting transfers between devices  17.4 us (11%)
    scatter-add x1, other arithmetic, body(): jnp.zeros((levels, rows_here * cols_here), jnp.float32).at[:, targets]  51.2 us
    unnamed x18, local copies, waits for them, and re-layouts  19 us
    ppermute x4, waiting for transfers between devices, with_halo(): lax.ppermute(lax.slice_in_dim(block, 0, width, axis=dim), axis, backward)  18.4 us
    ppermute x4, waiting for transfers between devices, with_halo(): lax.ppermute(lax.slice_in_dim(block, block.shape[dim] - width, None, axis...  11.8 us
    sub x8, other arithmetic, one_pass(): layer_field[:, 1:-1, 1:-1] + flux_east[:, 1:-1, 1:]  10.6 us
    all_to_all x1, starting transfers between devices, body(): lax.all_to_all(held, 'lon', split_axis=2, concat_axis=2, tiled=True)  8.72 us
    slice x1, local copies, waits for them, and re-layouts, body(): weighted = at_owner[1] * (at_owner[0] - at_column) * usable  7.62 us
    ppermute x4, starting transfers between devices, with_halo(): lax.ppermute(lax.slice_in_dim(block, 0, width, axis=dim), axis, backward)  7.1 us
  transfers between devices with their start and end apart: 9, of which 6 were waited for; matrix products, arithmetic and copies ran while one was open for 3% of the time, Pallas kernels for 0%

commit v1 on v0

--- a/solution.py
+++ b/solution.py
@@ -4,6 +4,24 @@
 from jax.sharding import PartitionSpec as P
 
 PASSES = 8
+
+
+def rails_arrange(a0, axis_no, frame):
+    fresh = a0.shape
+    small = a0.reshape(*fresh[:axis_no], frame, fresh[axis_no] // frame, *fresh[axis_no + 1 :])
+    tile_out = jnp.moveaxis(small, axis_no, 0)
+    return tile_out
+
+
+def draft_kinds(vec, pos_dim):
+    vec = jnp.moveaxis(vec, 0, pos_dim)
+    state_next = vec.shape
+    reply = vec.reshape(
+        *state_next[:pos_dim],
+        state_next[pos_dim] * state_next[pos_dim + 1],
+        *state_next[pos_dim + 2 :]
+    )
+    return reply
 
 
 def with_halo(block, sides, width):
@@ -44,7 +62,24 @@
     limits = jnp.broadcast_to(send_count[0][:, None], (lon_count, capacity)).reshape(slots)
     usable = jnp.where(slot_index % capacity < limits, 1.0, 0.0).astype(jnp.float32)
     held = jnp.stack([obs_value[:, 0, :], obs_weight[:, 0, :]])
-    at_owner = lax.all_to_all(held, "lon", split_axis=2, concat_axis=2, tiled=True)
+
+    def bind_yards_on(x_local, net_axis, load, w_in):
+        response = lax.axis_size(net_axis)
+        b_now = lax.axis_index(net_axis)
+        piece_next, carry_out = (response, b_now)
+        parts_out = rails_arrange(x_local, load, piece_next)
+        log = [parts_out[carry_out]]
+        for dev_j in range(1, piece_next):
+            after = parts_out[carry_out ^ dev_j]
+            log.append(
+                lax.ppermute(after, net_axis, [(pp, pp ^ dev_j) for pp in range(piece_next)])
+            )
+        s_next = jnp.stack(log, axis=0)
+        parts_out = s_next[carry_out ^ jnp.arange(piece_next)]
+        wide_out = draft_kinds(parts_out, w_in)
+        return wide_out
+
+    at_owner = bind_yards_on(held, "lon", 2, 2)
     at_column = jnp.take(columns, targets, axis=1)
     weighted = at_owner[1] * (at_owner[0] - at_column) * usable
     sea = land_sea.astype(jnp.float32)

time: 153 us -> 131 us (0.86)
  the two profiles are of different devices: /device:TPU:32 before, /device:TPU:1 now
where the time goes in v1:
time: 131 us
  starting transfers between devices  46.2 us (35%)
  other arithmetic  44 us (34%)
  local copies, waits for them, and re-layouts  26 us (20%)
  waiting for transfers between devices  13.9 us (11%)
    ppermute x15, starting transfers between devices, bind_yards_on(): lax.ppermute(after, net_axis, [(pp, pp ^ dev_j) for pp in range(piece_nex...  32.4 us
    scatter-add x1, other arithmetic, body(): jnp.zeros((levels, rows_here * cols_here), jnp.float32).at[:, targets]  24.7 us
    gather x2, local copies, waits for them, and re-layouts, body(): at_column = jnp.take(columns, targets, axis=1)  13.5 us
    sub x8, other arithmetic, one_pass(): layer_field[:, 1:-1, 1:-1] + flux_east[:, 1:-1, 1:]  10.6 us
    ppermute x4, starting transfers between devices, with_halo(): lax.ppermute(lax.slice_in_dim(block, 0, width, axis=dim), axis, backward)  8.96 us
    ppermute x4, waiting for transfers between devices, with_halo(): lax.ppermute(lax.slice_in_dim(block, block.shape[dim] - width, None, axis...  7.07 us
    unnamed x49, local copies, waits for them, and re-layouts  6.08 us
    ppermute x4, starting transfers between devices, with_halo(): lax.ppermute(lax.slice_in_dim(block, block.shape[dim] - width, None, axis...  4.91 us
  transfers between devices with their start and end apart: 23, of which 8 were waited for; matrix products, arithmetic and copies ran while one was open for 17% of the time, Pallas kernels for 0%

profile of v1, /device:TPU:1, one launch (start us, length us, event | category | flops | bytes accessed | tf_op | source)
XLA Modules:
  0.0 130.8 jit_solution(12651162301048609951)
XLA Ops:
  0.0 1.6 %reduce = f32[16,4096]{1,0:T(8,128)S(1)} reduce(f32[16,1,4096]{2,1,0:T(1,128)} %param.14, f32[]{:T(128)} %constant.87), dimensions={1}, to_apply=%param.14.reduce_sub_computation | reduce | bytes 524292 | tf_op args[6]
  1.9 0.6 reduce.1
  2.9 0.8 dynamic-slice_bitcast_fusion
  3.8 3.3 %collective-permute-start = (f32[2,16,256]{2,1,0:T(8,128)}, f32[2,16,256]{2,1,0:T(8,128)}, u32[]{:S(2)}, u32[]{:S(2)}) collective-permute-start(f32[2,16,256]{2,1,0:T(8,128)} %get-tuple-element.25), channel_id=1, source_target_pairs={{0,16},{16,0},{32,48},{48,32},{64,80},{80,64},{96,112},{112,96},{1... | collective-permute-start | bytes 98312 | tf_op jit(solution)/shard_map/ppermute | solution.py:75
  7.1 1.7 %collective-permute-start.2 = (f32[2,16,256]{2,1,0:T(8,128)}, f32[2,16,256]{2,1,0:T(8,128)}, u32[]{:S(2)}, u32[]{:S(2)}) collective-permute-start(f32[2,16,256]{2,1,0:T(8,128)} %get-tuple-element.23), channel_id=1, source_target_pairs={{0,48},{16,32},{32,16},{48,0},{64,112},{80,96},{96,80},{112,64},{1... | collective-permute-start | bytes 98312 | tf_op jit(solution)/shard_map/ppermute | solution.py:75
  9.0 0.5 collective-permute-start.20
  9.6 0.6 fusion.26
  10.2 0.5 collective-permute-done.19
  10.7 1.8 %collective-permute-done.20 = f32[3,32,8]{2,1,0:T(8,128)S(1)} collective-permute-done((f32[3,32,8]{2,1,0:T(8,128)S(1)}, f32[3,32,8]{2,1,0:T(8,128)S(1)}, u32[]{:S(2)}, u32[]{:S(2)}) %collective-permute-start.20) | collective-permute-done | bytes 3104 | tf_op jit(solution)/shard_map/ppermute | solution.py:36
  12.6 1.3 collective-permute-start.21
  13.8 3.7 %collective-permute-start.22 = (f32[3,8,272]{2,1,0:T(8,128)S(1)}, f32[3,8,272]{2,1,0:T(8,128)}, u32[]{:S(2)}, u32[]{:S(2)}) collective-permute-start(f32[3,8,272]{2,1,0:T(8,128)S(1)} %get-tuple-element.27), channel_id=1, source_target_pairs={{1,0},{2,1},{3,2},{4,3},{5,4},{6,5},{7,6},{8,7},{9,8},{10,9},{11,1... | collective-permute-start | bytes 78344 | tf_op jit(solution)/shard_map/ppermute | solution.py:36
  17.6 2.6 %copy.27 = f32[16,32,256]{0,2,1:T(8,128)} copy(f32[16,32,256]{2,1,0:T(8,128)S(1)} %copy-done.1) | data formatting | bytes 1048576 | tf_op args[0]
  20.2 13.0 %gather_fusion.1 = f32[4096,16]{1,0:T(8,128)S(1)} fusion(f32[16,8192]{0,1:T(8,128)} %bitcast.115, s32[4096]{0:T(1024)S(1)} %broadcast_clamp_fusion), kind=kCustom, calls=%fused_computation.1 | custom fusion | bytes 540672 | tf_op jit(solution)/shard_map/jit(_take)/gather | solution.py:83
  33.2 0.6 copy.28
  33.8 3.1 %collective-permute-start.3 = (f32[2,16,256]{2,1,0:T(8,128)}, f32[2,16,256]{2,1,0:T(8,128)S(1)}, u32[]{:S(2)}, u32[]{:S(2)}) collective-permute-start(f32[2,16,256]{2,1,0:T(8,128)} %get-tuple-element.22), channel_id=1, source_target_pairs={{0,64},{16,80},{32,96},{48,112},{64,0},{80,16},{96,32},{112,48},{1... | collective-permute-start | bytes 98312 | tf_op jit(solution)/shard_map/ppermute | solution.py:75
  36.9 2.4 %collective-permute-start.4 = (f32[2,16,256]{2,1,0:T(8,128)}, f32[2,16,256]{2,1,0:T(8,128)S(1)}, u32[]{:S(2)}, u32[]{:S(2)}) collective-permute-start(f32[2,16,256]{2,1,0:T(8,128)} %get-tuple-element.21), channel_id=1, source_target_pairs={{0,80},{16,64},{32,112},{48,96},{64,16},{80,0},{96,48},{112,32},{1... | collective-permute-start | bytes 98312 | tf_op jit(solution)/shard_map/ppermute | solution.py:75
  39.3 0.9 pad_maximum_fusion.1
  40.3 1.6 %collective-permute-start.5 = (f32[2,16,256]{2,1,0:T(8,128)}, f32[2,16,256]{2,1,0:T(8,128)S(1)}, u32[]{:S(2)}, u32[]{:S(2)}) collective-permute-start(f32[2,16,256]{2,1,0:T(8,128)} %get-tuple-element.20), channel_id=1, source_target_pairs={{0,96},{16,112},{32,64},{48,80},{64,32},{80,48},{96,0},{112,16},{1... | collective-permute-start | bytes 98312 | tf_op jit(solution)/shard_map/ppermute | solution.py:75
  41.8 0.8 constant_dynamic-update-slice_fusion.14
  42.6 2.5 %collective-permute-start.6 = (f32[2,16,256]{2,1,0:T(8,128)}, f32[2,16,256]{2,1,0:T(8,128)S(1)}, u32[]{:S(2)}, u32[]{:S(2)}) collective-permute-start(f32[2,16,256]{2,1,0:T(8,128)} %get-tuple-element.19), channel_id=1, source_target_pairs={{0,112},{16,96},{32,80},{48,64},{64,48},{80,32},{96,16},{112,0},{1... | collective-permute-start | bytes 98312 | tf_op jit(solution)/shard_map/ppermute | solution.py:75
  45.1 0.8 constant_dynamic-update-slice_fusion.13
  45.9 3.0 %collective-permute-start.7 = (f32[2,16,256]{2,1,0:T(8,128)}, f32[2,16,256]{2,1,0:T(8,128)S(1)}, u32[]{:S(2)}, u32[]{:S(2)}) collective-permute-start(f32[2,16,256]{2,1,0:T(8,128)} %get-tuple-element.18), channel_id=1, source_target_pairs={{0,128},{16,144},{32,160},{48,176},{64,192},{80,208},{96,224},{112... | collective-permute-start | bytes 98312 | tf_op jit(solution)/shard_map/ppermute | solution.py:75
  48.9 0.8 constant_dynamic-update-slice_fusion.12
  49.6 3.0 %collective-permute-start.8 = (f32[2,16,256]{2,1,0:T(8,128)}, f32[2,16,256]{2,1,0:T(8,128)S(1)}, u32[]{:S(2)}, u32[]{:S(2)}) collective-permute-start(f32[2,16,256]{2,1,0:T(8,128)} %get-tuple-element.17), channel_id=1, source_target_pairs={{0,144},{16,128},{32,176},{48,160},{64,208},{80,192},{96,240},{112... | collective-permute-start | bytes 98312 | tf_op jit(solution)/shard_map/ppermute | solution.py:75
  52.6 4.5 %collective-permute-start.10 = (f32[2,16,256]{2,1,0:T(8,128)}, f32[2,16,256]{2,1,0:T(8,128)S(1)}, u32[]{:S(2)}, u32[]{:S(2)}) collective-permute-start(f32[2,16,256]{2,1,0:T(8,128)} %get-tuple-element.15), channel_id=1, source_target_pairs={{0,176},{16,160},{32,144},{48,128},{64,240},{80,224},{96,208},{112... | collective-permute-start | bytes 98312 | tf_op jit(solution)/shard_map/ppermute | solution.py:75
  57.1 1.3 %collective-permute-start.11 = (f32[2,16,256]{2,1,0:T(8,128)S(1)}, f32[2,16,256]{2,1,0:T(8,128)S(1)}, u32[]{:S(2)}, u32[]{:S(2)}) collective-permute-start(f32[2,16,256]{2,1,0:T(8,128)S(1)} %copy-done.12), channel_id=1, source_target_pairs={{0,192},{16,208},{32,224},{48,240},{64,128},{80,144},{96,160},{112... | collective-permute-start | bytes 98312 | tf_op jit(solution)/shard_map/ppermute | solution.py:75
  58.5 3.1 %collective-permute-start.12 = (f32[2,16,256]{2,1,0:T(8,128)S(1)}, f32[2,16,256]{2,1,0:T(8,128)S(1)}, u32[]{:S(2)}, u32[]{:S(2)}) collective-permute-start(f32[2,16,256]{2,1,0:T(8,128)S(1)} %copy-done.11), channel_id=1, source_target_pairs={{0,208},{16,192},{32,240},{48,224},{64,144},{80,128},{96,176},{112... | collective-permute-start | bytes 98312 | tf_op jit(solution)/shard_map/ppermute | solution.py:75
  61.6 0.9 collective-permute-start.13
  62.5 2.0 %collective-permute-start.14 = (f32[2,16,256]{2,1,0:T(8,128)S(1)}, f32[2,16,256]{2,1,0:T(8,128)S(1)}, u32[]{:S(2)}, u32[]{:S(2)}) collective-permute-start(f32[2,16,256]{2,1,0:T(8,128)S(1)} %copy-done.9), channel_id=1, source_target_pairs={{0,240},{16,224},{32,208},{48,192},{64,176},{80,160},{96,144},{112... | collective-permute-start | bytes 98312 | tf_op jit(solution)/shard_map/ppermute | solution.py:75
  64.6 2.1 %collective-permute-done.13 = f32[2,16,256]{2,1,0:T(8,128)S(1)} collective-permute-done((f32[2,16,256]{2,1,0:T(8,128)S(1)}, f32[2,16,256]{2,1,0:T(8,128)S(1)}, u32[]{:S(2)}, u32[]{:S(2)}) %collective-permute-start.13) | collective-permute-done | bytes 32800 | tf_op jit(solution)/shard_map/ppermute | solution.py:75
  67.1 0.6 gather_fusion
  67.8 0.6 copy-done.5
  68.5 0.6 copy.29
  69.1 24.7 %scatter_custom_fusion = f32[16,8192]{0,1:T(8,128)} fusion(s32[4096]{0:T(1024)} %bitcast.133, f32[4096,16]{1,0:T(8,128)S(1)} %copy.29, f32[]{:T(128)} %constant.27.clone.1), kind=kCustom, calls=%fused_computation.3 | custom fusion | flops 65536 | bytes 524800 | tf_op jit(solution)/shard_map/scatter-add | solution.py:86
  93.7 2.9 %copy.30 = f32[16,32,256]{2,1,0:T(8,128)S(1)} copy(f32[16,32,256]{0,2,1:T(8,128)} %bitcast.114) | data formatting | bytes 1048576 | tf_op jit(solution)/shard_map/reshape | solution.py:87
  96.8 3.5 %collective-permute-start.15 = (f32[16,32,8]{2,1,0:T(8,128)S(1)}, f32[16,32,8]{2,1,0:T(8,128)S(1)}, u32[]{:S(2)}, u32[]{:S(2)}) collective-permute-start(f32[16,32,8]{2,1,0:T(8,128)S(1)} %get-tuple-element.7), channel_id=1, source_target_pairs={{0,16},{16,32},{32,48},{48,64},{64,80},{80,96},{96,112},{112,128},... | collective-permute-start | bytes 49160 | tf_op jit(solution)/shard_map/ppermute | solution.py:33
  100.6 3.0 %collective-permute-done.15 = f32[16,32,8]{2,1,0:T(8,128)S(1)} collective-permute-done((f32[16,32,8]{2,1,0:T(8,128)S(1)}, f32[16,32,8]{2,1,0:T(8,128)S(1)}, u32[]{:S(2)}, u32[]{:S(2)}) %collective-permute-start.15) | collective-permute-done | bytes 16416 | tf_op jit(solution)/shard_map/ppermute | solution.py:33
  103.6 2.5 %collective-permute-done.16 = f32[16,32,8]{2,1,0:T(8,128)S(1)} collective-permute-done((f32[16,32,8]{2,1,0:T(8,128)S(1)}, f32[16,32,8]{2,1,0:T(8,128)S(1)}, u32[]{:S(2)}, u32[]{:S(2)}) %collective-permute-start.16) | collective-permute-done | bytes 16416 | tf_op jit(solution)/shard_map/ppermute | solution.py:36
  106.4 4.8 %collective-permute-start.18 = (f32[16,8,272]{2,1,0:T(8,128)S(1)}, f32[16,8,272]{2,1,0:T(8,128)S(1)}, u32[]{:S(2)}, u32[]{:S(2)}) collective-permute-start(f32[16,8,272]{2,1,0:T(8,128)S(1)} %get-tuple-element.6), channel_id=1, source_target_pairs={{1,0},{2,1},{3,2},{4,3},{5,4},{6,5},{7,6},{8,7},{9,8},{10,9},{11,1... | collective-permute-start | bytes 417800 | tf_op jit(solution)/shard_map/ppermute | solution.py:36
  112.3 3.5 %collective-permute-done.17 = f32[16,8,272]{2,1,0:T(8,128)S(1)} collective-permute-done((f32[16,8,272]{2,1,0:T(8,128)S(1)}, f32[16,8,272]{2,1,0:T(8,128)S(1)}, u32[]{:S(2)}, u32[]{:S(2)}) %collective-permute-start.17) | collective-permute-done | bytes 139296 | tf_op jit(solution)/shard_map/ppermute | solution.py:33
  116.7 1.4 %slice_subtract_fusion.10 = f32[16,46,270]{2,1,0:T(8,128)S(1)} fusion(f32[16,47,272]{2,1,0:T(8,128)S(1)} %fusion.8, f32[16,48,271]{2,1,0:T(8,128)S(1)} %fusion.9, f32[16,48,272]{2,1,0:T(8,128)S(1)} %pad_maximum_fusion), kind=kLoop, calls=%fused_computation.25 | loop fusion | flops 794880 | bytes 4769280 | tf_op jit(solution)/shard_map/sub | solution.py:45
  118.7 1.4 %slice_subtract_fusion.6 = f32[16,44,268]{2,1,0:T(8,128)S(1)} fusion(f32[16,45,270]{2,1,0:T(8,128)S(1)} %fusion.6, f32[16,46,269]{2,1,0:T(8,128)S(1)} %fusion.7, f32[16,46,270]{2,1,0:T(8,128)S(1)} %slice_subtract_fusion.10), kind=kLoop, calls=%fused_computation.17 | loop fusion | flops 754688 | bytes 4528128 | tf_op jit(solution)/shard_map/sub | solution.py:45
  120.7 1.4 %slice_subtract_fusion.2 = f32[16,42,266]{2,1,0:T(8,128)S(1)} fusion(f32[16,43,268]{2,1,0:T(8,128)S(1)} %fusion.4, f32[16,44,267]{2,1,0:T(8,128)S(1)} %fusion.5, f32[16,44,268]{2,1,0:T(8,128)S(1)} %slice_subtract_fusion.6), kind=kLoop, calls=%fused_computation.9 | loop fusion | flops 715008 | bytes 4290048 | tf_op jit(solution)/shard_map/sub | solution.py:45
  122.7 1.2 slice_subtract_fusion.28
  124.3 1.2 slice_subtract_fusion.24
  126.0 1.2 slice_subtract_fusion.20
  127.7 1.2 slice_subtract_fusion.16
  129.4 1.5 %slice_subtract_fusion.30 = f32[16,32,256]{2,1,0:T(8,128)} fusion(f32[16,33,258]{2,1,0:T(8,128)S(1)} %fusion.10, f32[16,34,257]{2,1,0:T(8,128)S(1)} %fusion.11, f32[16,34,258]{2,1,0:T(8,128)S(1)} %slice_subtract_fusion.16), kind=kLoop, calls=%fused_computation.66 | loop fusion | flops 524288 | bytes 3145728 | tf_op jit(solution)/shard_map/sub | solution.py:45
  (118 shorter events, 7.7 us)
Async XLA Ops:
  0.0 9.5 %copy-start = (s32[1,16]{1,0:T(1,128)S(1)}, s32[1,16]{1,0:T(1,128)}, u32[]{:S(2)}) copy-start(s32[1,16]{1,0:T(1,128)} %param.13) | copy-start | bytes 196
  0.0 1.9 %copy-start.4 = (f32[16,1,4096]{2,1,0:T(1,128)S(1)}, f32[16,1,4096]{2,1,0:T(1,128)}, u32[]{:S(2)}) copy-start(f32[16,1,4096]{2,1,0:T(1,128)} %param.15) | copy-start | bytes 786436
  1.9 6.9 %copy-start.8 = (s32[32,256]{1,0:T(8,128)S(1)}, s32[32,256]{1,0:T(8,128)}, u32[]{:S(2)}) copy-start(s32[32,256]{1,0:T(8,128)} %param.11) | copy-start | bytes 98308
  2.6 6.2 %copy-start.2 = (f32[32,256]{1,0:T(8,128)S(1)}, f32[32,256]{1,0:T(8,128)}, u32[]{:S(2)}) copy-start(f32[32,256]{1,0:T(8,128)} %param.10) | copy-start | bytes 98308
  2.6 6.2 %copy-start.3 = (f32[32,256]{1,0:T(8,128)S(1)}, f32[32,256]{1,0:T(8,128)}, u32[]{:S(2)}) copy-start(f32[32,256]{1,0:T(8,128)} %param.9) | copy-start | bytes 98308
  2.7 6.8 %copy-start.6 = (s32[1,4096]{1,0:T(1,128)S(1)}, s32[1,4096]{1,0:T(1,128)}, u32[]{:S(2)}) copy-start(s32[1,4096]{1,0:T(1,128)} %param.12) | copy-start | bytes 49156
  2.8 14.8 %copy-start.1 = (f32[16,32,256]{2,1,0:T(8,128)S(1)}, f32[16,32,256]{2,1,0:T(8,128)}, u32[]{:S(2)}) copy-start(f32[16,32,256]{2,1,0:T(8,128)} %param.8) | copy-start | bytes 1572868
  3.8 36.5 %collective-permute-start = (f32[2,16,256]{2,1,0:T(8,128)}, f32[2,16,256]{2,1,0:T(8,128)}, u32[]{:S(2)}, u32[]{:S(2)}) collective-permute-start(f32[2,16,256]{2,1,0:T(8,128)} %get-tuple-element.25), channel_id=1, source_target_pairs={{0,16},{16,0},{32,48},{48,32},{64,80},{80,64},{96,112},{112,96},{1... | collective-permute-start | bytes 98312 | tf_op jit(solution)/shard_map/ppermute | solution.py:75
  7.0 35.5 %collective-permute-start.1 = (f32[2,16,256]{2,1,0:T(8,128)}, f32[2,16,256]{2,1,0:T(8,128)}, u32[]{:S(2)}, u32[]{:S(2)}) collective-permute-start(f32[2,16,256]{2,1,0:T(8,128)} %get-tuple-element.24), channel_id=1, source_target_pairs={{0,32},{16,48},{32,0},{48,16},{64,96},{80,112},{96,64},{112,80},{1... | collective-permute-start | bytes 98312 | tf_op jit(solution)/shard_map/ppermute | solution.py:75
  7.1 38.8 %collective-permute-start.2 = (f32[2,16,256]{2,1,0:T(8,128)}, f32[2,16,256]{2,1,0:T(8,128)}, u32[]{:S(2)}, u32[]{:S(2)}) collective-permute-start(f32[2,16,256]{2,1,0:T(8,128)} %get-tuple-element.23), channel_id=1, source_target_pairs={{0,48},{16,32},{32,16},{48,0},{64,112},{80,96},{96,80},{112,64},{1... | collective-permute-start | bytes 98312 | tf_op jit(solution)/shard_map/ppermute | solution.py:75
  8.9 1.8 %collective-permute-start.19 = (f32[3,32,8]{2,1,0:T(8,128)S(1)}, f32[3,32,8]{2,1,0:T(8,128)S(1)}, u32[]{:S(2)}, u32[]{:S(2)}) collective-permute-start(f32[3,32,8]{2,1,0:T(8,128)S(1)} %get-tuple-element.28), channel_id=1, source_target_pairs={{0,16},{16,32},{32,48},{48,64},{64,80},{80,96},{96,112},{112,128},... | collective-permute-start | bytes 9224 | tf_op jit(solution)/shard_map/ppermute | solution.py:33
  9.0 3.5 %collective-permute-start.20 = (f32[3,32,8]{2,1,0:T(8,128)S(1)}, f32[3,32,8]{2,1,0:T(8,128)S(1)}, u32[]{:S(2)}, u32[]{:S(2)}) collective-permute-start(f32[3,32,8]{2,1,0:T(8,128)S(1)} %get-tuple-element.29), channel_id=1, source_target_pairs={{16,0},{32,16},{48,32},{64,48},{80,64},{96,80},{112,96},{128,112},... | collective-permute-start | bytes 9224 | tf_op jit(solution)/shard_map/ppermute | solution.py:36
  9.5 10.7 %copy-start.7 = (s32[4096,1]{0,1:T(1,128)}, s32[4096,1]{0,1:T(1,128)S(1)}, u32[]{:S(2)}) copy-start(s32[4096,1]{0,1:T(1,128)S(1)} %compare_select_fusion) | copy-start | bytes 49156
  12.6 21.2 %collective-permute-start.21 = (f32[3,8,272]{2,1,0:T(8,128)S(1)}, f32[3,8,272]{2,1,0:T(8,128)S(1)}, u32[]{:S(2)}, u32[]{:S(2)}) collective-permute-start(f32[3,8,272]{2,1,0:T(8,128)S(1)} %get-tuple-element.26), channel_id=1, source_target_pairs={{0,1},{1,2},{2,3},{3,4},{4,5},{5,6},{6,7},{7,8},{8,9},{9,10},{10,1... | collective-permute-start | bytes 78344 | tf_op jit(solution)/shard_map/ppermute | solution.py:33
  13.8 23.0 %collective-permute-start.22 = (f32[3,8,272]{2,1,0:T(8,128)S(1)}, f32[3,8,272]{2,1,0:T(8,128)}, u32[]{:S(2)}, u32[]{:S(2)}) collective-permute-start(f32[3,8,272]{2,1,0:T(8,128)S(1)} %get-tuple-element.27), channel_id=1, source_target_pairs={{1,0},{2,1},{3,2},{4,3},{5,4},{6,5},{7,6},{8,7},{9,8},{10,9},{11,1... | collective-permute-start | bytes 78344 | tf_op jit(solution)/shard_map/ppermute | solution.py:36
  33.7 23.4 %copy-start.12 = (f32[2,16,256]{2,1,0:T(8,128)S(1)}, f32[2,16,256]{2,1,0:T(8,128)}, u32[]{:S(2)}) copy-start(f32[2,16,256]{2,1,0:T(8,128)} %get-tuple-element.14) | copy-start | bytes 98308
  33.7 24.7 %copy-start.11 = (f32[2,16,256]{2,1,0:T(8,128)S(1)}, f32[2,16,256]{2,1,0:T(8,128)}, u32[]{:S(2)}) copy-start(f32[2,16,256]{2,1,0:T(8,128)} %get-tuple-element.13) | copy-start | bytes 98308
  33.7 27.9 %copy-start.10 = (f32[2,16,256]{2,1,0:T(8,128)S(1)}, f32[2,16,256]{2,1,0:T(8,128)}, u32[]{:S(2)}) copy-start(f32[2,16,256]{2,1,0:T(8,128)} %get-tuple-element.12) | copy-start | bytes 98308
  33.7 28.7 %copy-start.9 = (f32[2,16,256]{2,1,0:T(8,128)S(1)}, f32[2,16,256]{2,1,0:T(8,128)}, u32[]{:S(2)}) copy-start(f32[2,16,256]{2,1,0:T(8,128)} %get-tuple-element.11) | copy-start | bytes 98308
  33.8 15.9 %collective-permute-start.3 = (f32[2,16,256]{2,1,0:T(8,128)}, f32[2,16,256]{2,1,0:T(8,128)S(1)}, u32[]{:S(2)}, u32[]{:S(2)}) collective-permute-start(f32[2,16,256]{2,1,0:T(8,128)} %get-tuple-element.22), channel_id=1, source_target_pairs={{0,64},{16,80},{32,96},{48,112},{64,0},{80,16},{96,32},{112,48},{1... | collective-permute-start | bytes 98312 | tf_op jit(solution)/shard_map/ppermute | solution.py:75
  36.9 15.7 %collective-permute-start.4 = (f32[2,16,256]{2,1,0:T(8,128)}, f32[2,16,256]{2,1,0:T(8,128)S(1)}, u32[]{:S(2)}, u32[]{:S(2)}) collective-permute-start(f32[2,16,256]{2,1,0:T(8,128)} %get-tuple-element.21), channel_id=1, source_target_pairs={{0,80},{16,64},{32,112},{48,96},{64,16},{80,0},{96,48},{112,32},{1... | collective-permute-start | bytes 98312 | tf_op jit(solution)/shard_map/ppermute | solution.py:75
  40.3 12.3 %collective-permute-start.5 = (f32[2,16,256]{2,1,0:T(8,128)}, f32[2,16,256]{2,1,0:T(8,128)S(1)}, u32[]{:S(2)}, u32[]{:S(2)}) collective-permute-start(f32[2,16,256]{2,1,0:T(8,128)} %get-tuple-element.20), channel_id=1, source_target_pairs={{0,96},{16,112},{32,64},{48,80},{64,32},{80,48},{96,0},{112,16},{1... | collective-permute-start | bytes 98312 | tf_op jit(solution)/shard_map/ppermute | solution.py:75
  42.6 14.5 %collective-permute-start.6 = (f32[2,16,256]{2,1,0:T(8,128)}, f32[2,16,256]{2,1,0:T(8,128)S(1)}, u32[]{:S(2)}, u32[]{:S(2)}) collective-permute-start(f32[2,16,256]{2,1,0:T(8,128)} %get-tuple-element.19), channel_id=1, source_target_pairs={{0,112},{16,96},{32,80},{48,64},{64,48},{80,32},{96,16},{112,0},{1... | collective-permute-start | bytes 98312 | tf_op jit(solution)/shard_map/ppermute | solution.py:75
  45.9 12.6 %collective-permute-start.7 = (f32[2,16,256]{2,1,0:T(8,128)}, f32[2,16,256]{2,1,0:T(8,128)S(1)}, u32[]{:S(2)}, u32[]{:S(2)}) collective-permute-start(f32[2,16,256]{2,1,0:T(8,128)} %get-tuple-element.18), channel_id=1, source_target_pairs={{0,128},{16,144},{32,160},{48,176},{64,192},{80,208},{96,224},{112... | collective-permute-start | bytes 98312 | tf_op jit(solution)/shard_map/ppermute | solution.py:75
  49.6 12.0 %collective-permute-start.8 = (f32[2,16,256]{2,1,0:T(8,128)}, f32[2,16,256]{2,1,0:T(8,128)S(1)}, u32[]{:S(2)}, u32[]{:S(2)}) collective-permute-start(f32[2,16,256]{2,1,0:T(8,128)} %get-tuple-element.17), channel_id=1, source_target_pairs={{0,144},{16,128},{32,176},{48,160},{64,208},{80,192},{96,240},{112... | collective-permute-start | bytes 98312 | tf_op jit(solution)/shard_map/ppermute | solution.py:75
  52.6 9.9 %collective-permute-start.9 = (f32[2,16,256]{2,1,0:T(8,128)}, f32[2,16,256]{2,1,0:T(8,128)S(1)}, u32[]{:S(2)}, u32[]{:S(2)}) collective-permute-start(f32[2,16,256]{2,1,0:T(8,128)} %get-tuple-element.16), channel_id=1, source_target_pairs={{0,160},{16,176},{32,128},{48,144},{64,224},{80,240},{96,192},{112... | collective-permute-start | bytes 98312 | tf_op jit(solution)/shard_map/ppermute | solution.py:75
  52.6 11.9 %collective-permute-start.10 = (f32[2,16,256]{2,1,0:T(8,128)}, f32[2,16,256]{2,1,0:T(8,128)S(1)}, u32[]{:S(2)}, u32[]{:S(2)}) collective-permute-start(f32[2,16,256]{2,1,0:T(8,128)} %get-tuple-element.15), channel_id=1, source_target_pairs={{0,176},{16,160},{32,144},{48,128},{64,240},{80,224},{96,208},{112... | collective-permute-start | bytes 98312 | tf_op jit(solution)/shard_map/ppermute | solution.py:75
  57.1 7.4 %collective-permute-start.11 = (f32[2,16,256]{2,1,0:T(8,128)S(1)}, f32[2,16,256]{2,1,0:T(8,128)S(1)}, u32[]{:S(2)}, u32[]{:S(2)}) collective-permute-start(f32[2,16,256]{2,1,0:T(8,128)S(1)} %copy-done.12), channel_id=1, source_target_pairs={{0,192},{16,208},{32,224},{48,240},{64,128},{80,144},{96,160},{112... | collective-permute-start | bytes 98312 | tf_op jit(solution)/shard_map/ppermute | solution.py:75
  58.5 6.2 %collective-permute-start.12 = (f32[2,16,256]{2,1,0:T(8,128)S(1)}, f32[2,16,256]{2,1,0:T(8,128)S(1)}, u32[]{:S(2)}, u32[]{:S(2)}) collective-permute-start(f32[2,16,256]{2,1,0:T(8,128)S(1)} %copy-done.11), channel_id=1, source_target_pairs={{0,208},{16,192},{32,240},{48,224},{64,144},{80,128},{96,176},{112... | collective-permute-start | bytes 98312 | tf_op jit(solution)/shard_map/ppermute | solution.py:75
  61.6 5.1 %collective-permute-start.13 = (f32[2,16,256]{2,1,0:T(8,128)S(1)}, f32[2,16,256]{2,1,0:T(8,128)S(1)}, u32[]{:S(2)}, u32[]{:S(2)}) collective-permute-start(f32[2,16,256]{2,1,0:T(8,128)S(1)} %copy-done.10), channel_id=1, source_target_pairs={{0,224},{16,240},{32,192},{48,208},{64,160},{80,176},{96,128},{112... | collective-permute-start | bytes 98312 | tf_op jit(solution)/shard_map/ppermute | solution.py:75
  62.5 4.6 %collective-permute-start.14 = (f32[2,16,256]{2,1,0:T(8,128)S(1)}, f32[2,16,256]{2,1,0:T(8,128)S(1)}, u32[]{:S(2)}, u32[]{:S(2)}) collective-permute-start(f32[2,16,256]{2,1,0:T(8,128)S(1)} %copy-done.9), channel_id=1, source_target_pairs={{0,240},{16,224},{32,208},{48,192},{64,176},{80,160},{96,144},{112... | collective-permute-start | bytes 98312 | tf_op jit(solution)/shard_map/ppermute | solution.py:75
  67.7 0.7 copy-start.5
  96.8 6.8 %collective-permute-start.15 = (f32[16,32,8]{2,1,0:T(8,128)S(1)}, f32[16,32,8]{2,1,0:T(8,128)S(1)}, u32[]{:S(2)}, u32[]{:S(2)}) collective-permute-start(f32[16,32,8]{2,1,0:T(8,128)S(1)} %get-tuple-element.7), channel_id=1, source_target_pairs={{0,16},{16,32},{32,48},{48,64},{64,80},{80,96},{96,112},{112,128},... | collective-permute-start | bytes 49160 | tf_op jit(solution)/shard_map/ppermute | solution.py:33
  100.3 5.8 %collective-permute-start.16 = (f32[16,32,8]{2,1,0:T(8,128)S(1)}, f32[16,32,8]{2,1,0:T(8,128)S(1)}, u32[]{:S(2)}, u32[]{:S(2)}) collective-permute-start(f32[16,32,8]{2,1,0:T(8,128)S(1)} %get-tuple-element.8), channel_id=1, source_target_pairs={{16,0},{32,16},{48,32},{64,48},{80,64},{96,80},{112,96},{128,112},... | collective-permute-start | bytes 49160 | tf_op jit(solution)/shard_map/ppermute | solution.py:36
  106.3 9.5 %collective-permute-start.17 = (f32[16,8,272]{2,1,0:T(8,128)S(1)}, f32[16,8,272]{2,1,0:T(8,128)S(1)}, u32[]{:S(2)}, u32[]{:S(2)}) collective-permute-start(f32[16,8,272]{2,1,0:T(8,128)S(1)} %get-tuple-element.5), channel_id=1, source_target_pairs={{0,1},{1,2},{2,3},{3,4},{4,5},{5,6},{6,7},{7,8},{8,9},{9,10},{10,1... | collective-permute-start | bytes 417800 | tf_op jit(solution)/shard_map/ppermute | solution.py:33
  106.4 9.4 %collective-permute-start.18 = (f32[16,8,272]{2,1,0:T(8,128)S(1)}, f32[16,8,272]{2,1,0:T(8,128)S(1)}, u32[]{:S(2)}, u32[]{:S(2)}) collective-permute-start(f32[16,8,272]{2,1,0:T(8,128)S(1)} %get-tuple-element.6), channel_id=1, source_target_pairs={{1,0},{2,1},{3,2},{4,3},{5,4},{6,5},{7,6},{8,7},{9,8},{10,9},{11,1... | collective-permute-start | bytes 417800 | tf_op jit(solution)/shard_map/ppermute | solution.py:36
